TPU v7x, 512 devices: a whole 4x4x16 slice. The times are simulated.
512 devices in a mesh: seg: 32 (over z, core), row: 16 (over x, y).
Axes of the slice: x: 4, y: 4, z: 16, core: 2. Of those that a mesh axis runs over, the one named last changes fastest.
Arguments:
- basis: bfloat16 [32, 8192, 1024], P('seg', 'row'), may hold values from -6 to 6
- arriving: bfloat16 [8192, 1024], P('row'), may hold values from -6 to 6
- blocks: bfloat16 [32, 8192, 256], P('seg', 'row'), may hold values from -8 to 8
- pattern: int32 [32, 128, 4], P('seg', 'row'), may hold values from 0 to 127, as said below
- growth: float32 [32, 1024], P('seg'), may hold values from -6 to 6
Outputs:
- next_basis: bfloat16 [32, 8192, 1024], P('seg', 'row')
- next_growth: float32 [32, 1024], P('seg')
Inputs may be any that keep to these rules, and one draw needn't show every extreme that they name: `pattern`: entry 0 of block row r is r itself; entry 1 is the block 4 positions before or after r on the cycle of 128 blocks; the other entries are distinct blocks fewer than 4 positions from r and not r.
All inputs are finite; a program needn't handle non-finite values.
Results may differ from a plain program's by a relative error of at most 0.0053.
Values may be sent and summed in bfloat16 or wider, within the bound.
No kernel may reach another device: no remote copies, remote signals or barrier semaphores. Data moves between devices by JAX's collectives and lax.ppermute only.
A program may use at most 128 MiB of HBM per device.

v0:
```python
import jax
import jax.numpy as jnp
from jax import lax
from jax.sharding import PartitionSpec as P

BS = 64
NB = 4
REACH = 4


def padded_2(block, sides, width):
    for axis, dim in sides:
        count = lax.axis_size(axis)
        forward = [(i, i + 1) for i in range(count - 1)]
        forward.append((count - 1, 0))
        backward = [(target, source) for source, target in forward]
        low = lax.ppermute(
            lax.slice_in_dim(block, block.shape[dim] - width, None, axis=dim), axis, forward
        )
        high = lax.ppermute(lax.slice_in_dim(block, 0, width, axis=dim), axis, backward)
        block = jnp.concatenate([low, block, high], axis=dim)
    return block


def shifted(array, axis, by):
    length = lax.axis_size(axis)
    pairs = [(i, i + by) for i in range(length) if 0 <= i + by < length]
    return lax.ppermute(array, axis, pairs)


def body(basis, arriving, blocks, pattern, growth):
    row_count = basis.shape[1]
    col_count = basis.shape[2]
    row_blocks = row_count // BS
    total_blocks = row_blocks * lax.axis_size("row")
    padded = padded_2(basis[0], (("row", 0),), REACH * BS)
    tile_stack = padded.reshape(row_blocks + 2 * REACH, BS, col_count)
    local_ids = jnp.arange(row_blocks, dtype=jnp.int32)
    own_blocks = lax.axis_index("row") * row_blocks + local_ids
    offsets = (pattern[0] - own_blocks[:, None] + REACH) % total_blocks
    picked = jnp.take(tile_stack, local_ids[:, None] + offsets, axis=0)
    values = blocks[0].reshape(row_blocks, BS, NB, BS)
    propagated = jnp.einsum("rinj,rnjk->rik", values, picked, preferred_element_type=jnp.float32)
    propagated = propagated.reshape(row_count, col_count).astype(jnp.bfloat16)
    partial_value = lax.dot_general(
        propagated, propagated, (((0,), (0,)), ((), ())), preferred_element_type=jnp.float32
    )
    gram_matrix = lax.psum(partial_value, "row")
    gram_matrix = gram_matrix / (row_count * lax.axis_size("row"))
    factor = jnp.linalg.cholesky(gram_matrix)
    next_growth = growth + jnp.log(jnp.diagonal(factor))[None, :]
    wide_rows = propagated.astype(jnp.float32)
    first_section = lax.axis_index("seg") == 0
    renewed = lax.linalg.triangular_solve(
        factor, wide_rows, left_side=False, lower=True, transpose_a=True
    )
    received = shifted(renewed.astype(jnp.bfloat16)[None], "seg", 1)
    next_basis = jnp.where(first_section, arriving[None], received)
    return (next_basis, next_growth)


def solution(mesh):
    return jax.shard_map(
        body,
        mesh=mesh,
        in_specs=(
            P("seg", "row", None),
            P("row", None),
            P("seg", "row", None),
            P("seg", "row", None),
            P("seg", None),
        ),
        out_specs=(P("seg", "row", None), P("seg", None)),
        check_vma=False,
    )
```

profile of v0, /device:TPU:1, one launch (start us, length us, event | category | flops | bytes accessed | tf_op | source)
XLA Modules:
  0.0 577.8 jit_solution(9313028965769077689)
XLA Ops:
  8.5 4.0 collective-permute-start
  12.5 5.6 collective-permute-start.1
  28.3 3.5 bitcast_convert_fusion
  31.8 3.3 convolution_bitcast_fusion
  35.5 143.7 %all-reduce.3.cloned.1.call-done = f32[1024,1024]{0,1:T(8,128)} async-done(((f32[1024,1024]{0,1:T(8,128)}), f32[1024,1024]{0,1:T(8,128)}) %all-reduce.3.cloned.1.call-update) | async-done | bytes 4194320 | tf_op jit(solution)/shard_map/psum | solution.py:48
  179.2 5.0 broadcast_multiply_fusion
  184.2 5.8 %copy.19 = f32[1024,1024]{1,0:T(8,128)} copy(f32[1024,1024]{0,1:T(8,128)} %broadcast_multiply_fusion) | data formatting | bytes 8388608 | tf_op jit(solution)/shard_map/div | solution.py:49
  190.0 4.4 fusion
  196.4 11.7 %cholesky.223 = f32[128,128]{1,0:T(8,128)S(1)} custom-call(f32[128,128]{1,0:T(8,128)S(1)} %cholesky.580), custom_call_target="Cholesky" | custom-call | tf_op jit(solution)/shard_map/jit(cholesky)/cholesky | solution.py:50
  208.2 9.8 %custom-call.62 = f32[1,128,128]{1,2,0:T(8,128)S(1)} custom-call(f32[1,128,128]{2,1,0:T(8,128)S(1)} %get-tuple-element.66), custom_call_target="InvertDiagBlocksLowerTriangular" | custom-call | tf_op jit(solution)/shard_map/jit(cholesky)/cholesky | solution.py:50
  224.4 11.9 %cholesky.244 = f32[128,128]{1,0:T(8,128)S(1)} custom-call(f32[128,128]{1,0:T(8,128)S(1)} %cholesky.584), custom_call_target="Cholesky" | custom-call | tf_op jit(solution)/shard_map/jit(cholesky)/cholesky | solution.py:50
  236.9 9.8 %custom-call.63 = f32[1,128,128]{1,2,0:T(8,128)S(1)} custom-call(f32[1,128,128]{2,1,0:T(8,128)S(1)} %get-tuple-element.63), custom_call_target="InvertDiagBlocksLowerTriangular" | custom-call | tf_op jit(solution)/shard_map/jit(cholesky)/cholesky | solution.py:50
  250.1 11.7 %cholesky.468 = f32[128,128]{1,0:T(8,128)S(1)} custom-call(f32[128,128]{1,0:T(8,128)S(1)} %cholesky.589), custom_call_target="Cholesky" | custom-call | tf_op jit(solution)/shard_map/jit(cholesky)/cholesky | solution.py:50
  263.1 9.8 %custom-call.64 = f32[1,128,128]{1,2,0:T(8,128)S(1)} custom-call(f32[1,128,128]{2,1,0:T(8,128)S(1)} %get-tuple-element.60), custom_call_target="InvertDiagBlocksLowerTriangular" | custom-call | tf_op jit(solution)/shard_map/jit(cholesky)/cholesky | solution.py:50
  276.4 11.9 %cholesky.487 = f32[128,128]{1,0:T(8,128)S(1)} custom-call(f32[128,128]{1,0:T(8,128)S(1)} %cholesky.594), custom_call_target="Cholesky" | custom-call | tf_op jit(solution)/shard_map/jit(cholesky)/cholesky | solution.py:50
  289.6 9.8 %custom-call.65 = f32[1,128,128]{1,2,0:T(8,128)S(1)} custom-call(f32[1,128,128]{2,1,0:T(8,128)S(1)} %get-tuple-element.57), custom_call_target="InvertDiagBlocksLowerTriangular" | custom-call | tf_op jit(solution)/shard_map/jit(cholesky)/cholesky | solution.py:50
  302.9 11.7 %cholesky.506 = f32[128,128]{1,0:T(8,128)S(1)} custom-call(f32[128,128]{1,0:T(8,128)S(1)} %cholesky.599), custom_call_target="Cholesky" | custom-call | tf_op jit(solution)/shard_map/jit(cholesky)/cholesky | solution.py:50
  316.0 10.2 %custom-call.66 = f32[1,128,128]{1,2,0:T(8,128)S(1)} custom-call(f32[1,128,128]{2,1,0:T(8,128)S(1)} %get-tuple-element.54), custom_call_target="InvertDiagBlocksLowerTriangular" | custom-call | tf_op jit(solution)/shard_map/jit(cholesky)/cholesky | solution.py:50
  329.5 11.7 %cholesky.526 = f32[128,128]{1,0:T(8,128)S(1)} custom-call(f32[128,128]{1,0:T(8,128)S(1)} %cholesky.604), custom_call_target="Cholesky" | custom-call | tf_op jit(solution)/shard_map/jit(cholesky)/cholesky | solution.py:50
  342.5 9.8 %custom-call.67 = f32[1,128,128]{1,2,0:T(8,128)S(1)} custom-call(f32[1,128,128]{2,1,0:T(8,128)S(1)} %get-tuple-element.51), custom_call_target="InvertDiagBlocksLowerTriangular" | custom-call | tf_op jit(solution)/shard_map/jit(cholesky)/cholesky | solution.py:50
  355.3 11.9 %cholesky.546 = f32[128,128]{1,0:T(8,128)S(1)} custom-call(f32[128,128]{1,0:T(8,128)S(1)} %cholesky.609), custom_call_target="Cholesky" | custom-call | tf_op jit(solution)/shard_map/jit(cholesky)/cholesky | solution.py:50
  368.4 9.8 %custom-call.68 = f32[1,128,128]{1,2,0:T(8,128)S(1)} custom-call(f32[1,128,128]{2,1,0:T(8,128)S(1)} %get-tuple-element.48), custom_call_target="InvertDiagBlocksLowerTriangular" | custom-call | tf_op jit(solution)/shard_map/jit(cholesky)/cholesky | solution.py:50
  380.9 11.7 %cholesky.564 = f32[128,128]{1,0:T(8,128)S(1)} custom-call(f32[128,128]{1,0:T(8,128)S(1)} %convolution_subtract_fusion.13), custom_call_target="Cholesky" | custom-call | tf_op jit(solution)/shard_map/jit(cholesky)/cholesky | solution.py:50
  399.5 6.6 %fusion.1 = (f32[1024,1024]{1,0:T(8,128)}, f32[1024,1024]{1,0:T(8,128)}) fusion(f32[1024,1024]{1,0:T(8,128)} %get-tuple-element.46, pred[]{:T(512)S(6)} %cholesky.579), kind=kLoop, calls=%fused_computation.8 | loop fusion | flops 4194304 | bytes 12582913 | tf_op jit(solution)/shard_map/triangular_solve | solution.py:54
  406.2 27.3 %while.1 = (s32[]{:T(128)}, f32[1024,1024]{1,0:T(8,128)}, s32[8,2]{0,1:T(2,128)S(1)}, f32[8,128,128]{2,1,0:T(8,128)}, s32[]{:T(128)}) while((s32[]{:T(128)}, f32[1024,1024]{1,0:T(8,128)}, s32[8,2]{0,1:T(2,128)S(1)}, f32[8,128,128]{2,1,0:T(8,128)}, s32[]{:T(128)}) %tuple.61), condition=%wide.while_cond, body=%wide.while_body.sunk | while | flops 2 | bytes 132205 | solution.py:54
  427.3 2.8 bitcast_dynamic-update-slice_fusion.9
  433.4 79.6 %custom-call.69 = f32[8,128,128]{1,2,0:T(8,128)S(1)} custom-call(f32[8,128,128]{2,1,0:T(8,128)} %get-tuple-element.9), custom_call_target="InvertDiagBlocksLowerTriangular" | custom-call | tf_op jit(solution)/shard_map/triangular_solve | solution.py:54
  528.3 3.2 convolution_subtract_fusion.4
  533.6 3.6 convolution_subtract_fusion.7
  539.2 4.3 convolution_subtract_fusion.3
  545.5 4.1 collective-permute-start.2
  550.1 17.3 %gather_fusion.1 = f32[1024]{0:T(1024)S(1)} fusion(f32[1024,1024]{1,0:T(8,128)} %get-tuple-element.23, s32[1024]{0:T(1024)S(1)} %bitcast.159), kind=kCustom, calls=%fused_computation.1 | custom fusion | bytes 16384 | tf_op jit(solution)/shard_map/jit(diagonal)/cond/branch_0_fun/gather | solution.py:51
  (115 shorter events, 98.0 us)
Async XLA Ops:
  7.2 172.0 %all-reduce.3.cloned.1.call-start = ((), (), s32[]{:S(2)}) async-start(), calls=%async_computation | async-start | bytes 8388608 | tf_op jit(solution)/shard_map/psum | solution.py:48
  8.5 14.2 %collective-permute-start = (bf16[256,1024]{1,0:T(8,128)(2,1)S(1)}, bf16[256,1024]{1,0:T(8,128)(2,1)S(1)}, u32[]{:S(2)}, u32[]{:S(2)}) collective-permute-start(bf16[256,1024]{1,0:T(8,128)(2,1)S(1)} %get-tuple-element.26), channel_id=1, source_target_pairs={{0,1},{1,2},{2,3},{3,4},{4,5},{5,6},{6,7},{7,8},{8,9},{9,10},{10,1... | collective-permute-start | bytes 1572872 | tf_op jit(solution)/shard_map/ppermute | solution.py:17
  12.5 11.7 %collective-permute-start.1 = (bf16[256,1024]{1,0:T(8,128)(2,1)S(1)}, bf16[256,1024]{1,0:T(8,128)(2,1)S(1)}, u32[]{:S(2)}, u32[]{:S(2)}) collective-permute-start(bf16[256,1024]{1,0:T(8,128)(2,1)S(1)} %get-tuple-element.27), channel_id=1, source_target_pairs={{1,0},{2,1},{3,2},{4,3},{5,4},{6,5},{7,6},{8,7},{9,8},{10,9},{11,1... | collective-permute-start | bytes 1572872 | tf_op jit(solution)/shard_map/ppermute | solution.py:20
  31.8 3.3 copy-start.1
  194.5 1.9 copy-start
  513.0 13.8 %copy-start.3 = (f32[8,128,128]{1,2,0:T(8,128)}, f32[8,128,128]{1,2,0:T(8,128)S(1)}, u32[]{:S(2)}) copy-start(f32[8,128,128]{1,2,0:T(8,128)S(1)} %custom-call.69) | copy-start | bytes 1572868
  531.6 18.0 %copy-start.2 = (bf16[512,1024]{1,0:T(8,128)(2,1)S(1)}, bf16[512,1024]{1,0:T(8,128)(2,1)}, u32[]{:S(2)}) copy-start(bf16[512,1024]{1,0:T(8,128)(2,1)} %param.6) | copy-start | bytes 3145732
  543.5 23.9 %copy-start.4 = (f32[1,1024]{1,0:T(1,128)S(1)}, f32[1,1024]{1,0:T(1,128)}, u32[]{:S(2)}) copy-start(f32[1,1024]{1,0:T(1,128)} %param.9) | copy-start | bytes 12292
  545.5 22.6 %collective-permute-start.2 = (bf16[1,512,1024]{1,2,0:T(8,128)(2,1)}, bf16[1,512,1024]{1,2,0:T(8,128)(2,1)}, u32[]{:S(2)}, u32[]{:S(2)}) collective-permute-start(bf16[1,512,1024]{1,2,0:T(8,128)(2,1)} %fusion.9), channel_id=1, source_target_pairs={{0,16},{16,32},{32,48},{48,64},{64,80},{80,96},{96,112},{112,128},... | collective-permute-start | bytes 3145736 | tf_op jit(solution)/shard_map/ppermute | solution.py:28
Sparse Core Ops, SparseCore 0:
  35.2 143.8 all-reduce.2
where the time goes:
time: 584 us; the launch traced here: 578 us
  other arithmetic  273 us (47%)
  waiting for transfers between devices  146 us (25%)
  local copies, waits for them, and re-layouts  63.6 us (11%)
  matrix products  61.6 us (11%)
  between operations  19.7 us (3%)
  starting transfers between devices  13.7 us (2%)
    another operation x30, other arithmetic, body(): factor = jnp.linalg.cholesky(gram_matrix)  172 us
    psum x1, waiting for transfers between devices, body(): gram_matrix = lax.psum(partial_value, 'row')  144 us
    another operation x3, other arithmetic, body(): lax.linalg.triangular_solve(factor, wide_rows, left_side=False, lower=Tru...  86.2 us
    another operation x15, matrix products, body(): lax.linalg.triangular_solve(factor, wide_rows, left_side=False, lower=Tru...  31.8 us
    another operation x24, local copies, waits for them, and re-layouts  27.3 us
    another operation x14, matrix products, body(): factor = jnp.linalg.cholesky(gram_matrix)  23.1 us
    gather x1, local copies, waits for them, and re-layouts, body(): next_growth = growth + jnp.log(jnp.diagonal(factor))[None, :]  17.3 us
  transfers between devices with their start and end apart: 4, of which 3 were waited for; matrix products, arithmetic and copies ran while one was open for 4% of the time, Pallas kernels for 0%

commit v1 on v0

--- a/solution.py
+++ b/solution.py
@@ -45,7 +45,7 @@
     partial_value = lax.dot_general(
         propagated, propagated, (((0,), (0,)), ((), ())), preferred_element_type=jnp.float32
     )
-    gram_matrix = lax.psum(partial_value, "row")
+    gram_matrix = jnp.sum(lax.all_gather(partial_value, "row"), axis=0)
     gram_matrix = gram_matrix / (row_count * lax.axis_size("row"))
     factor = jnp.linalg.cholesky(gram_matrix)
     next_growth = growth + jnp.log(jnp.diagonal(factor))[None, :]

time: 584 us -> 851 us (1.46)
  waiting for transfers between devices: 146 us -> 396 us
  other arithmetic: 273 us -> 291 us
    all_gather x0 -> x1, waiting for transfers between devices: none -> 393 us  [body(): gram_matrix = jnp.sum(lax.all_gather(partial_value, 'row'), axis=0)]
    psum x1 -> x0, waiting for transfers between devices: 144 us -> none  [body(): gram_matrix = lax.psum(partial_value, 'row')]
    reduce_sum x0 -> x1, other arithmetic: none -> 22.9 us  [body(): gram_matrix = jnp.sum(lax.all_gather(partial_value, 'row'), axis=0)]
  transfers between devices with their start and end apart: 4 -> 4, of which waited for: 3 -> 3; matrix products, arithmetic and copies ran while one was open for 4% -> 3% of each run, Pallas kernels for 0% -> 0%
where the time goes in v1:
time: 851 us; the launch traced here: 845 us
  waiting for transfers between devices  396 us (47%)
  other arithmetic  291 us (34%)
  local copies, waits for them, and re-layouts  63.6 us (7%)
  matrix products  61.6 us (7%)
  between operations  19.7 us (2%)
  starting transfers between devices  13.5 us (2%)
    all_gather x1, waiting for transfers between devices, body(): gram_matrix = jnp.sum(lax.all_gather(partial_value, 'row'), axis=0)  393 us
    another operation x30, other arithmetic, body(): factor = jnp.linalg.cholesky(gram_matrix)  172 us
    another operation x3, other arithmetic, body(): lax.linalg.triangular_solve(factor, wide_rows, left_side=False, lower=Tru...  86.2 us
    another operation x15, matrix products, body(): lax.linalg.triangular_solve(factor, wide_rows, left_side=False, lower=Tru...  31.8 us
    another operation x24, local copies, waits for them, and re-layouts  27.3 us
    another operation x14, matrix products, body(): factor = jnp.linalg.cholesky(gram_matrix)  23 us
    reduce_sum x1, other arithmetic, body(): gram_matrix = jnp.sum(lax.all_gather(partial_value, 'row'), axis=0)  22.9 us
    gather x1, local copies, waits for them, and re-layouts, body(): next_growth = growth + jnp.log(jnp.diagonal(factor))[None, :]  17.3 us
  transfers between devices with their start and end apart: 4, of which 3 were waited for; matrix products, arithmetic and copies ran while one was open for 3% of the time, Pallas kernels for 0%

profile of v1, /device:TPU:1, one launch (start us, length us, event | category | flops | bytes accessed | tf_op | source)
XLA Modules:
  0.0 845.2 jit_solution(17009992846806434591)
XLA Ops:
  8.5 4.0 collective-permute-start
  12.5 5.6 collective-permute-start.1
  28.3 3.5 bitcast_convert_fusion
  31.8 3.3 convolution_bitcast_fusion
  35.4 393.4 %all-gather.3.cloned.1.call-done = f32[16384,1024]{1,0:T(8,128)} async-done(((f32[1024,1024]{1,0:T(8,128)}), f32[16384,1024]{1,0:T(8,128)}) %all-gather.3.cloned.1.call-update) | async-done | bytes 67108880 | tf_op jit(solution)/shard_map/all_gather | solution.py:48
  428.9 22.9 %reduce_sum.11 = f32[1024,1024]{1,0:T(8,128)} reduce(f32[16,1024,1024]{2,1,0:T(8,128)} %bitcast.13, f32[]{:T(128)} %constant.318.clone.1), dimensions={0}, to_apply=%region_0.1 | reduce | flops 15728640 | bytes 71303168 | tf_op jit(solution)/shard_map/reduce_sum | solution.py:48
  451.8 5.8 copy.23
  457.7 4.4 fusion
  464.1 11.7 %cholesky.223 = f32[128,128]{1,0:T(8,128)S(1)} custom-call(f32[128,128]{1,0:T(8,128)S(1)} %cholesky.580), custom_call_target="Cholesky" | custom-call | tf_op jit(solution)/shard_map/jit(cholesky)/cholesky | solution.py:50
  478.3 9.8 %custom-call.62 = f32[1,128,128]{1,2,0:T(8,128)S(1)} custom-call(f32[1,128,128]{2,1,0:T(8,128)S(1)} %get-tuple-element.68), custom_call_target="InvertDiagBlocksLowerTriangular" | custom-call | tf_op jit(solution)/shard_map/jit(cholesky)/cholesky | solution.py:50
  492.0 11.9 %cholesky.244 = f32[128,128]{1,0:T(8,128)S(1)} custom-call(f32[128,128]{1,0:T(8,128)S(1)} %cholesky.584), custom_call_target="Cholesky" | custom-call | tf_op jit(solution)/shard_map/jit(cholesky)/cholesky | solution.py:50
  504.5 9.8 %custom-call.63 = f32[1,128,128]{1,2,0:T(8,128)S(1)} custom-call(f32[1,128,128]{2,1,0:T(8,128)S(1)} %get-tuple-element.65), custom_call_target="InvertDiagBlocksLowerTriangular" | custom-call | tf_op jit(solution)/shard_map/jit(cholesky)/cholesky | solution.py:50
  517.7 11.7 %cholesky.468 = f32[128,128]{1,0:T(8,128)S(1)} custom-call(f32[128,128]{1,0:T(8,128)S(1)} %cholesky.589), custom_call_target="Cholesky" | custom-call | tf_op jit(solution)/shard_map/jit(cholesky)/cholesky | solution.py:50
  530.7 9.8 %custom-call.64 = f32[1,128,128]{1,2,0:T(8,128)S(1)} custom-call(f32[1,128,128]{2,1,0:T(8,128)S(1)} %get-tuple-element.62), custom_call_target="InvertDiagBlocksLowerTriangular" | custom-call | tf_op jit(solution)/shard_map/jit(cholesky)/cholesky | solution.py:50
  544.1 11.9 %cholesky.487 = f32[128,128]{1,0:T(8,128)S(1)} custom-call(f32[128,128]{1,0:T(8,128)S(1)} %cholesky.594), custom_call_target="Cholesky" | custom-call | tf_op jit(solution)/shard_map/jit(cholesky)/cholesky | solution.py:50
  557.3 9.8 %custom-call.65 = f32[1,128,128]{1,2,0:T(8,128)S(1)} custom-call(f32[1,128,128]{2,1,0:T(8,128)S(1)} %get-tuple-element.59), custom_call_target="InvertDiagBlocksLowerTriangular" | custom-call | tf_op jit(solution)/shard_map/jit(cholesky)/cholesky | solution.py:50
  570.5 11.7 %cholesky.506 = f32[128,128]{1,0:T(8,128)S(1)} custom-call(f32[128,128]{1,0:T(8,128)S(1)} %cholesky.599), custom_call_target="Cholesky" | custom-call | tf_op jit(solution)/shard_map/jit(cholesky)/cholesky | solution.py:50
  583.6 10.2 %custom-call.66 = f32[1,128,128]{1,2,0:T(8,128)S(1)} custom-call(f32[1,128,128]{2,1,0:T(8,128)S(1)} %get-tuple-element.56), custom_call_target="InvertDiagBlocksLowerTriangular" | custom-call | tf_op jit(solution)/shard_map/jit(cholesky)/cholesky | solution.py:50
  597.1 11.7 %cholesky.526 = f32[128,128]{1,0:T(8,128)S(1)} custom-call(f32[128,128]{1,0:T(8,128)S(1)} %cholesky.604), custom_call_target="Cholesky" | custom-call | tf_op jit(solution)/shard_map/jit(cholesky)/cholesky | solution.py:50
  610.1 9.8 %custom-call.67 = f32[1,128,128]{1,2,0:T(8,128)S(1)} custom-call(f32[1,128,128]{2,1,0:T(8,128)S(1)} %get-tuple-element.53), custom_call_target="InvertDiagBlocksLowerTriangular" | custom-call | tf_op jit(solution)/shard_map/jit(cholesky)/cholesky | solution.py:50
  622.9 11.9 %cholesky.546 = f32[128,128]{1,0:T(8,128)S(1)} custom-call(f32[128,128]{1,0:T(8,128)S(1)} %cholesky.609), custom_call_target="Cholesky" | custom-call | tf_op jit(solution)/shard_map/jit(cholesky)/cholesky | solution.py:50
  636.0 9.8 %custom-call.68 = f32[1,128,128]{1,2,0:T(8,128)S(1)} custom-call(f32[1,128,128]{2,1,0:T(8,128)S(1)} %get-tuple-element.50), custom_call_target="InvertDiagBlocksLowerTriangular" | custom-call | tf_op jit(solution)/shard_map/jit(cholesky)/cholesky | solution.py:50
  648.5 11.7 %cholesky.564 = f32[128,128]{1,0:T(8,128)S(1)} custom-call(f32[128,128]{1,0:T(8,128)S(1)} %convolution_subtract_fusion.13), custom_call_target="Cholesky" | custom-call | tf_op jit(solution)/shard_map/jit(cholesky)/cholesky | solution.py:50
  667.1 6.6 fusion.1
  673.7 27.3 %while.1 = (s32[]{:T(128)}, f32[1024,1024]{1,0:T(8,128)}, s32[8,2]{0,1:T(2,128)S(1)}, f32[8,128,128]{2,1,0:T(8,128)}, s32[]{:T(128)}) while((s32[]{:T(128)}, f32[1024,1024]{1,0:T(8,128)}, s32[8,2]{0,1:T(2,128)S(1)}, f32[8,128,128]{2,1,0:T(8,128)}, s32[]{:T(128)}) %tuple.62), condition=%wide.while_cond, body=%wide.while_body.sunk | while | flops 2 | bytes 132705 | solution.py:54
  691.4 2.8 bitcast_dynamic-update-slice_fusion.9
  701.0 79.6 %custom-call.69 = f32[8,128,128]{1,2,0:T(8,128)S(1)} custom-call(f32[8,128,128]{2,1,0:T(8,128)} %get-tuple-element.9), custom_call_target="InvertDiagBlocksLowerTriangular" | custom-call | tf_op jit(solution)/shard_map/triangular_solve | solution.py:54
  795.9 3.2 convolution_subtract_fusion.4
  801.2 3.6 convolution_subtract_fusion.7
  806.8 4.3 convolution_subtract_fusion.3
  813.0 3.9 collective-permute-start.2
  817.5 17.3 %gather_fusion.1 = f32[1024]{0:T(1024)S(1)} fusion(f32[1024,1024]{1,0:T(8,128)} %get-tuple-element.25, s32[1024]{0:T(1024)S(1)} %bitcast.160), kind=kCustom, calls=%fused_computation.1 | custom fusion | bytes 16384 | tf_op jit(solution)/shard_map/jit(diagonal)/cond/branch_0_fun/gather | solution.py:51
  (115 shorter events, 98.0 us)
Async XLA Ops:
  7.2 421.7 %all-gather.3.cloned.1.call-start = ((), (), s32[]{:S(2)}) async-start(), calls=%async_computation | async-start | bytes 71303168 | tf_op jit(solution)/shard_map/all_gather | solution.py:48
  8.5 14.2 %collective-permute-start = (bf16[256,1024]{1,0:T(8,128)(2,1)S(1)}, bf16[256,1024]{1,0:T(8,128)(2,1)S(1)}, u32[]{:S(2)}, u32[]{:S(2)}) collective-permute-start(bf16[256,1024]{1,0:T(8,128)(2,1)S(1)} %get-tuple-element.28), channel_id=1, source_target_pairs={{0,1},{1,2},{2,3},{3,4},{4,5},{5,6},{6,7},{7,8},{8,9},{9,10},{10,1... | collective-permute-start | bytes 1572872 | tf_op jit(solution)/shard_map/ppermute | solution.py:17
  12.5 11.7 %collective-permute-start.1 = (bf16[256,1024]{1,0:T(8,128)(2,1)S(1)}, bf16[256,1024]{1,0:T(8,128)(2,1)S(1)}, u32[]{:S(2)}, u32[]{:S(2)}) collective-permute-start(bf16[256,1024]{1,0:T(8,128)(2,1)S(1)} %get-tuple-element.29), channel_id=1, source_target_pairs={{1,0},{2,1},{3,2},{4,3},{5,4},{6,5},{7,6},{8,7},{9,8},{10,9},{11,1... | collective-permute-start | bytes 1572872 | tf_op jit(solution)/shard_map/ppermute | solution.py:20
  31.8 3.3 copy-start.1
  462.1 1.9 copy-start
  780.6 13.8 %copy-start.3 = (f32[8,128,128]{1,2,0:T(8,128)}, f32[8,128,128]{1,2,0:T(8,128)S(1)}, u32[]{:S(2)}) copy-start(f32[8,128,128]{1,2,0:T(8,128)S(1)} %custom-call.69) | copy-start | bytes 1572868
  799.1 17.8 %copy-start.2 = (bf16[512,1024]{1,0:T(8,128)(2,1)S(1)}, bf16[512,1024]{1,0:T(8,128)(2,1)}, u32[]{:S(2)}) copy-start(bf16[512,1024]{1,0:T(8,128)(2,1)} %param.6) | copy-start | bytes 3145732
  811.1 23.7 %copy-start.4 = (f32[1,1024]{1,0:T(1,128)S(1)}, f32[1,1024]{1,0:T(1,128)}, u32[]{:S(2)}) copy-start(f32[1,1024]{1,0:T(1,128)} %param.9) | copy-start | bytes 12292
  813.0 22.4 %collective-permute-start.2 = (bf16[1,512,1024]{1,2,0:T(8,128)(2,1)}, bf16[1,512,1024]{1,2,0:T(8,128)(2,1)}, u32[]{:S(2)}, u32[]{:S(2)}) collective-permute-start(bf16[1,512,1024]{1,2,0:T(8,128)(2,1)} %fusion.9), channel_id=1, source_target_pairs={{0,16},{16,32},{32,48},{48,64},{64,80},{80,96},{96,112},{112,128},... | collective-permute-start | bytes 3145736 | tf_op jit(solution)/shard_map/ppermute | solution.py:28
Sparse Core Ops, SparseCore 0:
  35.2 393.6 all-gather.2
